TPU v7x, 128 devices: a whole 4x4x4 slice. The times are simulated.
128 devices in a mesh: segment: 2 (over core), tensor: 4 (over x), batch: 16 (over z, y).
Axes of the slice: x: 4, y: 4, z: 4, core: 2. Of those that a mesh axis runs over, the one named last changes fastest.
Arguments:
- hidden: bfloat16 [3, 128, 16384], P(None, 'tensor', 'batch'), may hold values from -6 to 6
- norm_gain: bfloat16 [2, 16384], P('segment', 'batch'), may hold values from 0.25 to 1.75
- w_query: bfloat16 [2, 16384, 8192], P('segment', 'batch', 'tensor'), may hold values from -0.046875 to 0.046875
- key_value_weight: bfloat16 [2, 16384, 2048], P('segment', 'batch', 'tensor'), may hold values from -0.046875 to 0.046875
- w_out: bfloat16 [2, 8192, 16384], P('segment', 'tensor', 'batch'), may hold values from -0.0625 to 0.0625
- key_value_cache: bfloat16 [2, 32, 8, 256, 256], P('segment', 'batch', 'tensor'), may hold values from -6 to 6
- owner_slot: int32 [32], replicated, may hold values from 0 to 31, each once
- accepted: int32 [3, 32], replicated, may hold values from 1 to 4
Outputs:
- layer_outputs: bfloat16 [2, 3, 128, 16384], P('segment', None, 'tensor', 'batch')
- new_cache: bfloat16 [2, 32, 8, 12, 256], P('segment', 'batch', 'tensor')
Inputs may be any that keep to these rules, and one draw needn't show every extreme that they name: `owner_slot`: each slot is held by exactly one request; slot s belongs to index s // 2 of batch.
All inputs are finite; a program needn't handle non-finite values.
Results may differ from a plain program's by a relative error of at most 0.0095.
Values may be sent and summed in bfloat16 or wider, within the bound.
No kernel may reach another device: no remote copies, remote signals or barrier semaphores. Data moves between devices by JAX's collectives and lax.ppermute only.
A program may use at most 64 MiB of HBM per device.

v0:
```python
import jax
import jax.numpy as jnp
from jax import lax
from jax.sharding import PartitionSpec as P

MODEL_WIDTH = 16384
HEAD_SIZE = 128
DRAFT_BLOCK = 4
DECODE_ROUNDS = 3
GROUP_HEADS = 8


def passed_along(block, axis, distance):
    devices = range(lax.axis_size(axis))
    route = [(i - distance, i) for i in devices if i - distance in devices]
    return lax.ppermute(block, axis, route)


def pass_on(rows):
    return passed_along(rows, "segment", 1)


def shards(
    hidden, norm_gain, w_query, key_value_weight, w_out, key_value_cache, owner_slot, accepted
):
    n_segment = lax.axis_size("segment")
    segment = lax.axis_index("segment")
    group = lax.axis_index("batch")
    requests = owner_slot.shape[0]
    slots = key_value_cache.shape[1]
    kv_local = key_value_cache.shape[2]
    query_cols = w_query.shape[2]
    own_rows = slots * DRAFT_BLOCK
    scale = HEAD_SIZE ** (-0.5)
    gain = norm_gain[0].astype(jnp.float32)
    cache_local = key_value_cache[0]
    onehot = (owner_slot[None, :] == jnp.arange(requests)[:, None]).astype(jnp.int32)
    inverse = jnp.sum(onehot * jnp.arange(requests)[None, :], axis=1)
    acc_slot = jnp.sum(onehot[None] * accepted[:, None, :], axis=2)
    acc_own = lax.dynamic_slice_in_dim(acc_slot, group * slots, slots, 1)
    sort_index = (inverse[:, None] * DRAFT_BLOCK + jnp.arange(DRAFT_BLOCK)[None, :]).reshape(-1)
    back_index = (owner_slot[:, None] * DRAFT_BLOCK + jnp.arange(DRAFT_BLOCK)[None, :]).reshape(-1)
    positions = jnp.arange(DECODE_ROUNDS * DRAFT_BLOCK)
    round_of = positions // DRAFT_BLOCK
    place = positions % DRAFT_BLOCK
    causal = jnp.arange(DRAFT_BLOCK)[None, :] <= jnp.arange(DRAFT_BLOCK)[:, None]
    ext = jnp.zeros((slots, kv_local, DECODE_ROUNDS * DRAFT_BLOCK, 2 * HEAD_SIZE), jnp.bfloat16)
    record = jnp.zeros((DECODE_ROUNDS,) + hidden.shape[1:], jnp.bfloat16)
    x = jnp.zeros(hidden.shape[1:], jnp.bfloat16)
    for rnd in range(DECODE_ROUNDS):
        for step in range(n_segment):
            if step == 0:
                x = jnp.where(segment == 0, hidden[rnd], x)
            layer_rnd = jnp.int32(rnd)
            xf = x.astype(jnp.float32)
            total = lax.psum(jnp.sum(xf * xf, axis=1), "batch")
            normed = (xf * lax.rsqrt(total / MODEL_WIDTH + 1e-05)[:, None] * gain[None, :]).astype(
                jnp.bfloat16
            )
            rows_all = lax.all_gather(normed, "tensor", axis=0, tiled=True)
            sorted_rows = jnp.take(rows_all, sort_index, axis=0)
            first = jnp.dot(sorted_rows, w_query[0], preferred_element_type=jnp.float32)
            second = jnp.dot(sorted_rows, key_value_weight[0], preferred_element_type=jnp.float32)
            proj = lax.psum_scatter(
                jnp.concatenate([first, second], axis=1), "batch", scatter_dimension=0, tiled=True
            )
            query_rows_new = proj[:, :query_cols].astype(jnp.bfloat16)
            key_value_rows = proj[:, query_cols:].astype(jnp.bfloat16)
            query_heads = query_rows_new.reshape(
                slots, DRAFT_BLOCK, kv_local, GROUP_HEADS, HEAD_SIZE
            )
            fresh_key_value = key_value_rows.reshape(
                slots, DRAFT_BLOCK, kv_local, 2 * HEAD_SIZE
            ).transpose(0, 2, 1, 3)
            keys_all = jnp.concatenate([cache_local, ext, fresh_key_value], axis=2)
            acc_by_pos = acc_own[round_of, :].T
            ext_valid = (round_of[None, :] < layer_rnd) & (place[None, :] < acc_by_pos)
            mask = jnp.concatenate(
                [
                    jnp.ones((slots, DRAFT_BLOCK, cache_local.shape[2]), bool),
                    jnp.broadcast_to(
                        ext_valid[:, None, :], (slots, DRAFT_BLOCK, DECODE_ROUNDS * DRAFT_BLOCK)
                    ),
                    jnp.broadcast_to(causal[None], (slots, DRAFT_BLOCK, DRAFT_BLOCK)),
                ],
                axis=2,
            )
            scores = (
                jnp.einsum(
                    "sjhgd,shld->shgjl",
                    query_heads,
                    keys_all[..., :HEAD_SIZE],
                    preferred_element_type=jnp.float32,
                )
                * scale
            )
            scores = jnp.where(mask[:, None, None], scores, -1e30)
            weights = jax.nn.softmax(scores, axis=-1).astype(jnp.bfloat16)
            attended = jnp.einsum(
                "shgjl,shld->sjhgd",
                weights,
                keys_all[..., HEAD_SIZE:],
                preferred_element_type=jnp.float32,
            )
            attended = attended.astype(jnp.bfloat16).reshape(own_rows, query_cols)
            partial_out = jnp.dot(
                lax.all_gather(attended, "batch", axis=0, tiled=True),
                w_out[0],
                preferred_element_type=jnp.float32,
            )
            unsorted = jnp.take(partial_out, back_index, axis=0)
            summed = lax.psum_scatter(
                unsorted.astype(jnp.bfloat16), "tensor", scatter_dimension=0, tiled=True
            ).astype(jnp.float32)
            x_new = (xf + summed).astype(jnp.bfloat16)
            acc_now = lax.dynamic_index_in_dim(acc_own, layer_rnd, 0, keepdims=False)
            keep = jnp.arange(DRAFT_BLOCK)[None, :] < acc_now[:, None]
            masked = jnp.where(
                keep[:, None, :, None], fresh_key_value, jnp.zeros_like(fresh_key_value)
            )
            ext_new = lax.dynamic_update_slice(ext, masked, (0, 0, layer_rnd * DRAFT_BLOCK, 0))
            x_new, ext_new = (x_new, ext_new)
            active = segment == step
            ext = jnp.where(active, ext_new, ext)
            record = record.at[rnd].set(jnp.where(active, x_new, record[rnd]))
            if step + 1 < n_segment:
                x = pass_on(x_new)
    return (record[None], ext[None])


def solution(mesh):
    in_specs = (
        P(None, "tensor", "batch"),
        P("segment", "batch"),
        P("segment", "batch", "tensor"),
        P("segment", "batch", "tensor"),
        P("segment", "tensor", "batch"),
        P("segment", "batch", "tensor", None, None),
        P(),
        P(),
    )
    out_specs = (P("segment", None, "tensor", "batch"), P("segment", "batch", "tensor", None, None))
    return jax.shard_map(shards, mesh=mesh, in_specs=in_specs, out_specs=out_specs, check_vma=False)
```

profile of v0, /device:TPU:0, one launch (start us, length us, event | category | flops | bytes accessed | tf_op | source)
XLA Modules:
  0.0 944.5 jit_solution(7901623505001223784)
XLA Ops:
  10.1 1.3 fusion.120
  13.7 1.0 fusion.92
  14.7 42.0 %psum.42 = f32[32]{0:T(128)S(1)} all-reduce(f32[32]{0:T(128)S(1)} %fusion.92), channel_id=1, replica_groups=mesh['segment'=2,'tensor'=4,'batch'=16] {'batch'}, use_global_device_ids=true, to_apply=%region_1.0 | all-reduce | flops 32 | bytes 256 | tf_op jit(solution)/shard_map/psum | solution.py:56
  56.8 0.9 fusion.94
  57.7 12.6 %all_gather.36 = bf16[128,1024]{1,0:T(8,128)(2,1)S(1)} all-gather(bf16[32,1024]{1,0:T(8,128)(2,1)S(1)} %fusion.94), channel_id=1, replica_groups=mesh['segment'=2,'tensor'=4,'batch'=16] {'tensor'}, dimensions={0}, use_global_device_ids=true | all-gather | bytes 327680 | tf_op jit(solution)/shard_map/all_gather | solution.py:60
  71.5 3.0 fusion.28
  74.6 82.2 %all-reduce.16 = bf16[128,2560]{1,0:T(8,128)(2,1)S(1)} all-reduce(f32[128,2560]{1,0:T(8,128)S(1)} %pad_maximum_fusion), channel_id=2, replica_groups=mesh['segment'=2,'tensor'=4,'batch'=16] {'batch'}, use_global_device_ids=true, to_apply=%region_3.5.clone | all-reduce | flops 327680 | bytes 1966080
  156.8 1.2 dynamic-slice.57
  159.7 0.9 multiply_reduce_fusion
  164.6 20.9 %all_gather.37 = bf16[128,2048]{1,0:T(8,128)(2,1)S(1)} all-gather(bf16[8,2048]{1,0:T(8,128)(2,1)S(1)} %reshape.476), channel_id=1, replica_groups=mesh['segment'=2,'tensor'=4,'batch'=16] {'batch'}, dimensions={0}, use_global_device_ids=true | all-gather | bytes 557056 | tf_op jit(solution)/shard_map/all_gather | solution.py:107
  185.6 2.9 fusion.16
  190.5 20.0 %reduce-scatter.7.cloned.1.call-done = bf16[32,1024]{1,0:T(8,128)(2,1)} async-done(((bf16[128,1024]{1,0:T(8,128)(2,1)}), bf16[32,1024]{1,0:T(8,128)(2,1)}) %reduce-scatter.7.cloned.1.call-update) | async-done | bytes 65552 | tf_op jit(solution)/shard_map/reduce_scatter | solution.py:112
  210.4 0.9 fusion.113
  211.3 1.3 collective-permute-start
  213.6 40.6 %all-reduce.11 = (f32[32]{0:T(128)S(1)}, f32[32]{0:T(128)S(1)}) all-reduce(f32[32]{0:T(128)S(1)} %get-tuple-element.111, f32[32]{0:T(128)S(1)} %get-tuple-element.102), channel_id=1, replica_groups=mesh['segment'=2,'tensor'=4,'batch'=16] {'batch'}, use_global_device_ids=true, to_apply=%region_9.12 | all-reduce | flops 64 | bytes 512 | tf_op jit(solution)/shard_map/psum | solution.py:56
  254.3 12.4 %all_gather.38 = bf16[128,1024]{1,0:T(8,128)(2,1)S(1)} all-gather(bf16[32,1024]{1,0:T(8,128)(2,1)S(1)} %get-tuple-element.115), channel_id=1, replica_groups=mesh['segment'=2,'tensor'=4,'batch'=16] {'tensor'}, dimensions={0}, use_global_device_ids=true | all-gather | bytes 327680 | tf_op jit(solution)/shard_map/all_gather | solution.py:60
  267.9 4.0 fusion.26
  271.9 12.2 %all_gather.40 = bf16[128,1024]{1,0:T(8,128)(2,1)S(1)} all-gather(bf16[32,1024]{1,0:T(8,128)(2,1)S(1)} %get-tuple-element.114), channel_id=1, replica_groups=mesh['segment'=2,'tensor'=4,'batch'=16] {'tensor'}, dimensions={0}, use_global_device_ids=true | all-gather | bytes 327680 | tf_op jit(solution)/shard_map/all_gather | solution.py:60
  285.3 3.0 fusion.24
  288.5 1.2 pad_maximum_fusion.2
  289.7 88.6 %all-reduce.17 = (bf16[128,2560]{1,0:T(8,128)(2,1)}, bf16[128,2560]{1,0:T(8,128)(2,1)}) all-reduce(f32[128,2560]{1,0:T(8,128)S(1)} %pad_maximum_fusion.1, f32[128,2560]{1,0:T(8,128)} %pad_maximum_fusion.2), channel_id=4, replica_groups=mesh['segment'=2,'tensor'=4,'batch'=16] {'batch'}, use_global_device_ids=true, to_apply=%region_10.13.clone | all-reduce | flops 655360 | bytes 3932160
  381.4 1.3 fusion.56
  382.7 21.0 %all_gather.41 = bf16[128,2048]{1,0:T(8,128)(2,1)S(1)} all-gather(bf16[8,2048]{1,0:T(8,128)(2,1)S(1)} %reshape.483), channel_id=1, replica_groups=mesh['segment'=2,'tensor'=4,'batch'=16] {'batch'}, dimensions={0}, use_global_device_ids=true | all-gather | bytes 557056 | tf_op jit(solution)/shard_map/all_gather | solution.py:107
  403.7 2.9 fusion.12
  408.3 24.3 %all_gather.39 = bf16[128,2048]{1,0:T(8,128)(2,1)S(1)} all-gather(bf16[8,2048]{1,0:T(8,128)(2,1)S(1)} %reshape.479), channel_id=1, replica_groups=mesh['segment'=2,'tensor'=4,'batch'=16] {'batch'}, dimensions={0}, use_global_device_ids=true | all-gather | bytes 557056 | tf_op jit(solution)/shard_map/all_gather | solution.py:107
  432.5 3.0 fusion.14
  436.4 0.9 select_convert_fusion.3
  438.8 16.3 %reduce-scatter.9.cloned.1.call-done = bf16[32,1024]{1,0:T(8,128)(2,1)} async-done(((bf16[128,1024]{1,0:T(8,128)(2,1)}), bf16[32,1024]{1,0:T(8,128)(2,1)}) %reduce-scatter.9.cloned.1.call-update) | async-done | bytes 65552 | tf_op jit(solution)/shard_map/reduce_scatter | solution.py:112
  455.1 0.9 fusion.110
  456.0 22.1 %reduce-scatter.11.cloned.1.call-done = bf16[32,1024]{1,0:T(8,128)(2,1)} async-done(((bf16[128,1024]{1,0:T(8,128)(2,1)}), bf16[32,1024]{1,0:T(8,128)(2,1)}) %reduce-scatter.11.cloned.1.call-update) | async-done | bytes 65552 | tf_op jit(solution)/shard_map/reduce_scatter | solution.py:112
  478.1 0.9 fusion.112
  479.0 1.3 collective-permute-start.1
  481.2 1.0 fusion.84
  482.1 40.6 %all-reduce.9 = (f32[32]{0:T(128)S(1)}, f32[32]{0:T(128)S(1)}) all-reduce(f32[32]{0:T(128)S(1)} %get-tuple-element.110, f32[32]{0:T(128)S(1)} %get-tuple-element.98), channel_id=1, replica_groups=mesh['segment'=2,'tensor'=4,'batch'=16] {'batch'}, use_global_device_ids=true, to_apply=%region_21.24 | all-reduce | flops 64 | bytes 512 | tf_op jit(solution)/shard_map/psum | solution.py:56
  522.9 12.3 %all_gather.42 = bf16[128,1024]{1,0:T(8,128)(2,1)S(1)} all-gather(bf16[32,1024]{1,0:T(8,128)(2,1)S(1)} %get-tuple-element.113), channel_id=1, replica_groups=mesh['segment'=2,'tensor'=4,'batch'=16] {'tensor'}, dimensions={0}, use_global_device_ids=true | all-gather | bytes 327680 | tf_op jit(solution)/shard_map/all_gather | solution.py:60
  535.1 1.0 gather_fusion.7
  536.5 4.0 fusion.22
  540.4 12.2 %all_gather.44 = bf16[128,1024]{1,0:T(8,128)(2,1)S(1)} all-gather(bf16[32,1024]{1,0:T(8,128)(2,1)S(1)} %get-tuple-element.112), channel_id=1, replica_groups=mesh['segment'=2,'tensor'=4,'batch'=16] {'tensor'}, dimensions={0}, use_global_device_ids=true | all-gather | bytes 327680 | tf_op jit(solution)/shard_map/all_gather | solution.py:60
  552.7 1.0 gather_fusion.9
  554.0 3.0 fusion.20
  557.2 1.2 pad_maximum_fusion.4
  558.3 88.6 %all-reduce.18 = (bf16[128,2560]{1,0:T(8,128)(2,1)}, bf16[128,2560]{1,0:T(8,128)(2,1)}) all-reduce(f32[128,2560]{1,0:T(8,128)S(1)} %pad_maximum_fusion.3, f32[128,2560]{1,0:T(8,128)} %pad_maximum_fusion.4), channel_id=8, replica_groups=mesh['segment'=2,'tensor'=4,'batch'=16] {'batch'}, use_global_device_ids=true, to_apply=%region_22.25.clone | all-reduce | flops 655360 | bytes 3932160
  650.1 1.3 fusion.58
  651.4 21.0 %all_gather.45 = bf16[128,2048]{1,0:T(8,128)(2,1)S(1)} all-gather(bf16[8,2048]{1,0:T(8,128)(2,1)S(1)} %reshape.490), channel_id=1, replica_groups=mesh['segment'=2,'tensor'=4,'batch'=16] {'batch'}, dimensions={0}, use_global_device_ids=true | all-gather | bytes 557056 | tf_op jit(solution)/shard_map/all_gather | solution.py:107
  672.4 3.0 fusion.8
  675.3 1.0 gather_fusion.10
  677.1 24.1 %all_gather.43 = bf16[128,2048]{1,0:T(8,128)(2,1)S(1)} all-gather(bf16[8,2048]{1,0:T(8,128)(2,1)S(1)} %reshape.486), channel_id=1, replica_groups=mesh['segment'=2,'tensor'=4,'batch'=16] {'batch'}, dimensions={0}, use_global_device_ids=true | all-gather | bytes 557056 | tf_op jit(solution)/shard_map/all_gather | solution.py:107
  701.2 3.0 fusion.10
  704.2 1.0 gather_fusion.8
  705.2 0.9 select_convert_fusion.1
  706.8 17.1 %reduce-scatter.13.cloned.1.call-done = bf16[32,1024]{1,0:T(8,128)(2,1)} async-done(((bf16[128,1024]{1,0:T(8,128)(2,1)}), bf16[32,1024]{1,0:T(8,128)(2,1)}) %reduce-scatter.13.cloned.1.call-update) | async-done | bytes 65552 | tf_op jit(solution)/shard_map/reduce_scatter | solution.py:112
  724.9 21.9 %reduce-scatter.15.cloned.1.call-done = bf16[32,1024]{1,0:T(8,128)(2,1)} async-done(((bf16[128,1024]{1,0:T(8,128)(2,1)}), bf16[32,1024]{1,0:T(8,128)(2,1)}) %reduce-scatter.15.cloned.1.call-update) | async-done | bytes 65552 | tf_op jit(solution)/shard_map/reduce_scatter | solution.py:112
  746.8 0.9 bitcast_dynamic-update-slice_fusion
  747.6 1.3 collective-permute-start.2
  749.9 40.5 %psum.47 = f32[32]{0:T(128)S(1)} all-reduce(f32[32]{0:T(128)S(1)} %fusion.88), channel_id=1, replica_groups=mesh['segment'=2,'tensor'=4,'batch'=16] {'batch'}, use_global_device_ids=true, to_apply=%region_33.36 | all-reduce | flops 32 | bytes 256 | tf_op jit(solution)/shard_map/psum | solution.py:56
  790.6 12.3 %all_gather.46 = bf16[128,1024]{1,0:T(8,128)(2,1)S(1)} all-gather(bf16[32,1024]{1,0:T(8,128)(2,1)S(1)} %fusion.90), channel_id=1, replica_groups=mesh['segment'=2,'tensor'=4,'batch'=16] {'tensor'}, dimensions={0}, use_global_device_ids=true | all-gather | bytes 327680 | tf_op jit(solution)/shard_map/all_gather | solution.py:60
  802.9 1.0 gather_fusion.11
  804.2 2.9 fusion.18
  807.3 82.3 %all-reduce.19 = bf16[128,2560]{1,0:T(8,128)(2,1)} all-reduce(f32[128,2560]{1,0:T(8,128)S(1)} %pad_maximum_fusion.5), channel_id=12, replica_groups=mesh['segment'=2,'tensor'=4,'batch'=16] {'batch'}, use_global_device_ids=true, to_apply=%region_34.37.clone | all-reduce | flops 327680 | bytes 1966080
  891.2 20.9 %all_gather.47 = bf16[128,2048]{1,0:T(8,128)(2,1)S(1)} all-gather(bf16[8,2048]{1,0:T(8,128)(2,1)S(1)} %reshape.493), channel_id=1, replica_groups=mesh['segment'=2,'tensor'=4,'batch'=16] {'batch'}, dimensions={0}, use_global_device_ids=true | all-gather | bytes 557056 | tf_op jit(solution)/shard_map/all_gather | solution.py:107
  912.2 2.9 fusion.6
  915.1 1.0 gather_fusion.12
  917.7 18.5 %reduce-scatter.17.cloned.1.call-done = bf16[32,1024]{1,0:T(8,128)(2,1)} async-done(((bf16[128,1024]{1,0:T(8,128)(2,1)}), bf16[32,1024]{1,0:T(8,128)(2,1)}) %reduce-scatter.17.cloned.1.call-update) | async-done | bytes 65552 | tf_op jit(solution)/shard_map/reduce_scatter | solution.py:112
  936.2 1.5 fusion.104
  (218 shorter events, 35.8 us)
Async XLA Ops:
  7.2 64.0 %copy-start = (bf16[1,1024,512]{2,1,0:T(8,128)(2,1)S(1)}, bf16[1,1024,512]{2,1,0:T(8,128)(2,1)}, u32[]{:S(2)}) copy-start(bf16[1,1024,512]{2,1,0:T(8,128)(2,1)} %param.27) | copy-start | bytes 3145732
  7.2 203.3 %reduce-scatter.7.cloned.1.call-start = ((), (), s32[]{:S(2)}) async-start(), calls=%async_computation.6 | async-start | bytes 327680 | tf_op jit(solution)/shard_map/reduce_scatter | solution.py:112
  70.3 213.8 %copy-start.16 = (s32[1024]{0:T(1024)}, s32[1024]{0:T(1024)S(1)}, u32[]{:S(2)}) copy-start(s32[1024]{0:T(1024)S(1)} %pad_clamp_fusion.2) | copy-start | bytes 12292
  74.6 88.5 %copy-start.1 = (bf16[1,2,2,256,256]{4,3,2,1,0:T(8,128)(2,1)S(1)}, bf16[1,2,2,256,256]{4,3,2,1,0:T(8,128)(2,1)}, u32[]{:S(2)}) copy-start(bf16[1,2,2,256,256]{4,3,2,1,0:T(8,128)(2,1)} %param.29) | copy-start | bytes 1572868
  156.8 6.3 copy-start.26
  158.9 277.4 %copy-start.18 = (pred[128]{0:T(512)(128)(4,1)}, pred[128]{0:T(512)(128)(4,1)S(1)}, u32[]{:S(2)}) copy-start(pred[128]{0:T(512)(128)(4,1)S(1)} %compare_and_fusion) | copy-start | bytes 388
  163.8 216.3 %copy-start.24 = (pred[2,4,272]{2,1,0:T(4,128)(4,1)}, pred[2,4,272]{2,1,0:T(4,128)(4,1)S(1)}, u32[]{:S(2)}) copy-start(pred[2,4,272]{2,1,0:T(4,128)(4,1)S(1)} %get-tuple-element.122) | copy-start | bytes 6532
  185.6 249.9 %copy-start.17 = (s32[1024]{0:T(1024)}, s32[1024]{0:T(1024)S(1)}, u32[]{:S(2)}) copy-start(s32[1024]{0:T(1024)S(1)} %pad_clamp_fusion) | copy-start | bytes 12292
  188.5 21.9 %copy-start.6 = (bf16[3,32,1024]{2,1,0:T(8,128)(2,1)S(1)}, bf16[3,32,1024]{2,1,0:T(8,128)(2,1)}, u32[]{:S(2)}) copy-start(bf16[3,32,1024]{2,1,0:T(8,128)(2,1)} %param.24) | copy-start | bytes 589828
  190.2 264.9 %reduce-scatter.9.cloned.1.call-start = ((), (), s32[]{:S(2)}) async-start(), calls=%async_computation.7 | async-start | bytes 327680 | tf_op jit(solution)/shard_map/reduce_scatter | solution.py:112
  211.3 2.2 collective-permute-start
  212.6 54.9 %copy-start.7 = (bf16[2,2,12,256]{3,2,1,0:T(8,128)(2,1)}, bf16[2,2,12,256]{3,2,1,0:T(8,128)(2,1)S(1)}, u32[]{:S(2)}) copy-start(bf16[2,2,12,256]{3,2,1,0:T(8,128)(2,1)S(1)} %pad_select_fusion) | copy-start | bytes 73732
  285.3 3.0 copy-start.2
  289.7 90.3 %copy-start.11 = (bf16[2,2,12,256]{3,2,1,0:T(8,128)(2,1)S(1)}, bf16[2,2,12,256]{3,2,1,0:T(8,128)(2,1)}, u32[]{:S(2)}) copy-start(bf16[2,2,12,256]{3,2,1,0:T(8,128)(2,1)} %copy-done.7) | copy-start | bytes 73732
  289.7 90.4 %copy-start.8 = (bf16[2,2,12,256]{3,2,1,0:T(8,128)(2,1)S(1)}, bf16[2,2,12,256]{3,2,1,0:T(8,128)(2,1)}, u32[]{:S(2)}) copy-start(bf16[2,2,12,256]{3,2,1,0:T(8,128)(2,1)} %copy-done.7) | copy-start | bytes 73732
  380.0 58.8 %copy-start.9 = (bf16[2,2,12,256]{3,2,1,0:T(8,128)(2,1)}, bf16[2,2,12,256]{3,2,1,0:T(8,128)(2,1)S(1)}, u32[]{:S(2)}) copy-start(bf16[2,2,12,256]{3,2,1,0:T(8,128)(2,1)S(1)} %fusion.121) | copy-start | bytes 73732
  380.1 0.8 copy-start.5
  437.3 40.8 %reduce-scatter.11.cloned.1.call-start = ((), (), s32[]{:S(2)}) async-start(), calls=%async_computation.8 | async-start | bytes 327680 | tf_op jit(solution)/shard_map/reduce_scatter | solution.py:112
  438.1 285.9 %reduce-scatter.13.cloned.1.call-start = ((), (), s32[]{:S(2)}) async-start(), calls=%async_computation.9 | async-start | bytes 327680 | tf_op jit(solution)/shard_map/reduce_scatter | solution.py:112
  438.8 96.3 %copy-start.21 = (pred[2,4]{1,0:T(4,128)(4,1)}, pred[2,4]{1,0:T(4,128)(4,1)S(1)}, u32[]{:S(2)}) copy-start(pred[2,4]{1,0:T(4,128)(4,1)S(1)} %get-tuple-element.133) | copy-start | bytes 28
  479.0 2.2 collective-permute-start.1
  480.4 54.8 %copy-start.13 = (bf16[2,2,12,256]{3,2,1,0:T(8,128)(2,1)}, bf16[2,2,12,256]{3,2,1,0:T(8,128)(2,1)S(1)}, u32[]{:S(2)}) copy-start(bf16[2,2,12,256]{3,2,1,0:T(8,128)(2,1)S(1)} %constant_dynamic-update-slice_fusion.1) | copy-start | bytes 73732
  554.0 3.0 copy-start.3
  558.3 90.3 %copy-start.10 = (bf16[2,2,12,256]{3,2,1,0:T(8,128)(2,1)S(1)}, bf16[2,2,12,256]{3,2,1,0:T(8,128)(2,1)}, u32[]{:S(2)}) copy-start(bf16[2,2,12,256]{3,2,1,0:T(8,128)(2,1)} %copy-done.9) | copy-start | bytes 73732
  558.3 90.3 %copy-start.12 = (bf16[2,2,12,256]{3,2,1,0:T(8,128)(2,1)S(1)}, bf16[2,2,12,256]{3,2,1,0:T(8,128)(2,1)}, u32[]{:S(2)}) copy-start(bf16[2,2,12,256]{3,2,1,0:T(8,128)(2,1)} %copy.173) | copy-start | bytes 73732
  558.3 90.3 %copy-start.22 = (pred[2,4]{1,0:T(4,128)(4,1)S(1)}, pred[2,4]{1,0:T(4,128)(4,1)}, u32[]{:S(2)}) copy-start(pred[2,4]{1,0:T(4,128)(4,1)} %copy-done.21) | copy-start | bytes 28
  558.3 90.4 %copy-start.14 = (bf16[2,2,12,256]{3,2,1,0:T(8,128)(2,1)S(1)}, bf16[2,2,12,256]{3,2,1,0:T(8,128)(2,1)}, u32[]{:S(2)}) copy-start(bf16[2,2,12,256]{3,2,1,0:T(8,128)(2,1)} %copy-done.13) | copy-start | bytes 73732
  647.0 2.7 copy-start.23
  648.8 0.8 copy-start.4
  675.3 1.0 copy-start.25
  704.2 1.0 copy-start.19
  705.2 43.8 %copy-start.20 = (pred[2,4]{1,0:T(4,128)(4,1)S(1)}, pred[2,4]{1,0:T(4,128)(4,1)}, u32[]{:S(2)}) copy-start(pred[2,4]{1,0:T(4,128)(4,1)} %get-tuple-element.132) | copy-start | bytes 28
  706.2 40.6 %reduce-scatter.15.cloned.1.call-start = ((), (), s32[]{:S(2)}) async-start(), calls=%async_computation.10 | async-start | bytes 327680 | tf_op jit(solution)/shard_map/reduce_scatter | solution.py:112
  706.8 229.4 %reduce-scatter.17.cloned.1.call-start = ((), (), s32[]{:S(2)}) async-start(), calls=%async_computation.11 | async-start | bytes 327680 | tf_op jit(solution)/shard_map/reduce_scatter | solution.py:112
  747.6 42.9 %copy-start.15 = (bf16[1,3,32,1024]{3,2,1,0:T(8,128)(2,1)}, bf16[1,3,32,1024]{3,2,1,0:T(8,128)(2,1)S(1)}, u32[]{:S(2)}) copy-start(bf16[1,3,32,1024]{3,2,1,0:T(8,128)(2,1)S(1)} %get-tuple-element.94) | copy-start | bytes 589828
  747.6 2.2 collective-permute-start.2
Sparse Core Ops, SparseCore 0:
  190.4 20.0 reduce-scatter.6
  437.5 17.6 reduce-scatter.8
  457.5 20.5 reduce-scatter.10
  706.3 17.6 reduce-scatter.12
  726.2 20.5 reduce-scatter.14
  917.1 19.0 reduce-scatter.16
where the time goes:
time: 947 us; the launch traced here: 945 us
  blocking collectives  712 us (75%)
  waiting for transfers between devices  119 us (13%)
  matrix products  44.8 us (5%)
  other arithmetic  28.4 us (3%)
  local copies, waits for them, and re-layouts  20.8 us (2%)
  between operations  15.8 us (2%)
    unnamed x4, blocking collectives  342 us
    psum x4, blocking collectives, shards(): total = lax.psum(jnp.sum(xf * xf, axis=1), 'batch')  164 us
    all_gather x6, blocking collectives, shards(): lax.all_gather(attended, 'batch', axis=0, tiled=True)  132 us
    reduce_scatter x6, waiting for transfers between devices, shards(): lax.psum_scatter(unsorted.astype(jnp.bfloat16), 'tensor', scatter_dimensi...  116 us
    all_gather x6, blocking collectives, shards(): rows_all = lax.all_gather(normed, 'tensor', axis=0, tiled=True)  74 us
    dot_general x6, matrix products, shards(): first = jnp.dot(sorted_rows, w_query[0], preferred_element_type=jnp.float32)  19.9 us
  transfers between devices with their start and end apart: 9, of which 9 were waited for; matrix products, arithmetic and copies ran while one was open for 0% of the time, Pallas kernels for 0%

commit v1 on v0

--- a/solution.py
+++ b/solution.py
@@ -8,6 +8,12 @@
 DRAFT_BLOCK = 4
 DECODE_ROUNDS = 3
 GROUP_HEADS = 8
+
+
+def measure_results(point, out_dim):
+    kept_arr = list(point.shape[1:])
+    kept_arr[out_dim] *= point.shape[0]
+    return jnp.moveaxis(point, 0, out_dim).reshape(kept_arr)
 
 
 def passed_along(block, axis, distance):
@@ -103,10 +109,33 @@
                 preferred_element_type=jnp.float32,
             )
             attended = attended.astype(jnp.bfloat16).reshape(own_rows, query_cols)
+
+            def test_copies(row_axis, a0, which_dim):
+                n_shards = lax.axis_size(row_axis)
+                seen = list(map(lambda b: (b, (b + 1) % n_shards), range(n_shards)))
+                row_list = [(idx, j) for j, idx in seen]
+                state_next, out_arr = ([], [])
+                ix = 0
+                while ix < n_shards - 1:
+                    if ix % 2 == 0:
+                        spare = lax.ppermute(
+                            state_next[-1] if state_next else a0, axis_name=row_axis, perm=seen
+                        )
+                        state_next.append(spare)
+                    else:
+                        out_arr.append(
+                            lax.ppermute(
+                                out_arr[-1] if out_arr else a0, axis_name=row_axis, perm=row_list
+                            )
+                        )
+                    ix += 1
+                r_now = jnp.stack([*state_next[::-1], a0, *out_arr])
+                piece_now = lax.axis_index(row_axis) - len(state_next)
+                r_now = r_now[(jnp.arange(n_shards) - piece_now) % n_shards]
+                return measure_results(r_now, which_dim)
+
             partial_out = jnp.dot(
-                lax.all_gather(attended, "batch", axis=0, tiled=True),
-                w_out[0],
-                preferred_element_type=jnp.float32,
+                test_copies("batch", attended, 0), w_out[0], preferred_element_type=jnp.float32
             )
             unsorted = jnp.take(partial_out, back_index, axis=0)
             summed = lax.psum_scatter(

time: 947 us -> 1080 us (1.14)
  starting transfers between devices: 4.12 us -> 185 us
  blocking collectives: 712 us -> 579 us
  waiting for transfers between devices: 119 us -> 179 us
  local copies, waits for them, and re-layouts: 20.8 us -> 37.8 us
    ppermute x0 -> x90, starting transfers between devices: none -> 181 us  [the longest x42 157 us: test_copies(): lax.ppermute(out_arr[-1] if out_arr else a0, axis_name=row_axis, perm=row...]
    all_gather x6 -> x0, blocking collectives: 132 us -> none  [shards(): lax.all_gather(attended, 'batch', axis=0, tiled=True)]
    ppermute x0 -> x90, waiting for transfers between devices: none -> 62.5 us  [the longest x48 62.3 us: test_copies(): lax.ppermute(state_next[-1] if state_next else a0, axis_name=row_axis, pe...]
  transfers between devices with their start and end apart: 9 -> 99, of which waited for: 9 -> 30; matrix products, arithmetic and copies ran while one was open for 0% -> 3% of each run, Pallas kernels for 0% -> 0%
where the time goes in v1:
time: 1080 us; the launch traced here: 1070 us
  blocking collectives  579 us (54%)
  starting transfers between devices  185 us (17%)
  waiting for transfers between devices  179 us (17%)
  matrix products  42.7 us (4%)
  local copies, waits for them, and re-layouts  37.8 us (3%)
  other arithmetic  29.1 us (3%)
  between operations  17 us (2%)
    unnamed x4, blocking collectives  341 us
    psum x4, blocking collectives, shards(): total = lax.psum(jnp.sum(xf * xf, axis=1), 'batch')  164 us
    ppermute x42, starting transfers between devices, test_copies(): lax.ppermute(out_arr[-1] if out_arr else a0, axis_name=row_axis, perm=row...  157 us
    reduce_scatter x6, waiting for transfers between devices, shards(): lax.psum_scatter(unsorted.astype(jnp.bfloat16), 'tensor', scatter_dimensi...  113 us
    all_gather x6, blocking collectives, shards(): rows_all = lax.all_gather(normed, 'tensor', axis=0, tiled=True)  74.1 us
    ppermute x48, waiting for transfers between devices, test_copies(): lax.ppermute(state_next[-1] if state_next else a0, axis_name=row_axis, pe...  62.3 us
    ppermute x48, starting transfers between devices, test_copies(): lax.ppermute(state_next[-1] if state_next else a0, axis_name=row_axis, pe...  23.7 us
  transfers between devices with their start and end apart: 99, of which 30 were waited for; matrix products, arithmetic and copies ran while one was open for 3% of the time, Pallas kernels for 0%

profile of v1, /device:TPU:0, one launch (start us, length us, event | category | flops | bytes accessed | tf_op | source)
XLA Modules:
  0.0 1070.1 jit_solution(11097109121845150013)
XLA Ops:
  14.6 42.0 %psum.42 = f32[32]{0:T(128)S(1)} all-reduce(f32[32]{0:T(128)S(1)} %fusion.98), channel_id=1, replica_groups=mesh['segment'=2,'tensor'=4,'batch'=16] {'batch'}, use_global_device_ids=true, to_apply=%region_1.0 | all-reduce | flops 32 | bytes 256 | tf_op jit(solution)/shard_map/psum | solution.py:62
  57.6 12.6 %all_gather.18 = bf16[128,1024]{1,0:T(8,128)(2,1)S(1)} all-gather(bf16[32,1024]{1,0:T(8,128)(2,1)S(1)} %fusion.100), channel_id=1, replica_groups=mesh['segment'=2,'tensor'=4,'batch'=16] {'tensor'}, dimensions={0}, use_global_device_ids=true | all-gather | bytes 327680 | tf_op jit(solution)/shard_map/all_gather | solution.py:66
  71.4 3.0 fusion.28
  74.5 82.1 %all-reduce.16 = bf16[128,2560]{1,0:T(8,128)(2,1)S(1)} all-reduce(f32[128,2560]{1,0:T(8,128)S(1)} %pad_maximum_fusion), channel_id=2, replica_groups=mesh['segment'=2,'tensor'=4,'batch'=16] {'batch'}, use_global_device_ids=true, to_apply=%region_3.5.clone | all-reduce | flops 327680 | bytes 1966080
  163.7 7.2 collective-permute-done
  170.9 5.3 collective-permute-start.8
  178.3 5.4 collective-permute-start.9
  185.4 5.6 collective-permute-start.10
  192.6 5.6 collective-permute-start.11
  199.9 5.6 collective-permute-start.12
  207.1 5.6 collective-permute-start.13
  214.4 5.5 collective-permute-start.14
  222.3 2.9 fusion.16
  227.8 20.6 %reduce-scatter.7.cloned.1.call-done = bf16[32,1024]{1,0:T(8,128)(2,1)} async-done(((bf16[128,1024]{1,0:T(8,128)(2,1)}), bf16[32,1024]{1,0:T(8,128)(2,1)}) %reduce-scatter.7.cloned.1.call-update) | async-done | bytes 65552 | tf_op jit(solution)/shard_map/reduce_scatter | solution.py:141
  251.7 40.6 %all-reduce.11 = (f32[32]{0:T(128)S(1)}, f32[32]{0:T(128)S(1)}) all-reduce(f32[32]{0:T(128)S(1)} %get-tuple-element.111, f32[32]{0:T(128)S(1)} %get-tuple-element.102), channel_id=1, replica_groups=mesh['segment'=2,'tensor'=4,'batch'=16] {'batch'}, use_global_device_ids=true, to_apply=%region_9.12 | all-reduce | flops 64 | bytes 512 | tf_op jit(solution)/shard_map/psum | solution.py:62
  292.3 12.5 %all_gather.19 = bf16[128,1024]{1,0:T(8,128)(2,1)S(1)} all-gather(bf16[32,1024]{1,0:T(8,128)(2,1)S(1)} %get-tuple-element.115), channel_id=1, replica_groups=mesh['segment'=2,'tensor'=4,'batch'=16] {'tensor'}, dimensions={0}, use_global_device_ids=true | all-gather | bytes 327680 | tf_op jit(solution)/shard_map/all_gather | solution.py:66
  306.1 4.0 fusion.26
  310.1 12.2 %all_gather.20 = bf16[128,1024]{1,0:T(8,128)(2,1)S(1)} all-gather(bf16[32,1024]{1,0:T(8,128)(2,1)S(1)} %get-tuple-element.114), channel_id=1, replica_groups=mesh['segment'=2,'tensor'=4,'batch'=16] {'tensor'}, dimensions={0}, use_global_device_ids=true | all-gather | bytes 327680 | tf_op jit(solution)/shard_map/all_gather | solution.py:66
  323.5 3.0 fusion.24
  327.9 88.9 %all-reduce.17 = (bf16[128,2560]{1,0:T(8,128)(2,1)}, bf16[128,2560]{1,0:T(8,128)(2,1)}) all-reduce(f32[128,2560]{1,0:T(8,128)S(1)} %pad_maximum_fusion.1, f32[128,2560]{1,0:T(8,128)} %pad_maximum_fusion.2), channel_id=4, replica_groups=mesh['segment'=2,'tensor'=4,'batch'=16] {'batch'}, use_global_device_ids=true, to_apply=%region_10.13.clone | all-reduce | flops 655360 | bytes 3932160
  420.4 6.4 collective-permute-done.31
  426.8 5.3 collective-permute-start.39
  434.3 5.5 collective-permute-start.40
  441.9 5.3 collective-permute-start.41
  449.3 5.3 collective-permute-start.42
  456.7 5.3 collective-permute-start.43
  464.3 5.3 collective-permute-start.44
  471.7 5.3 collective-permute-start.45
  480.0 5.1 collective-permute-done.23
  496.0 2.9 fusion.14
  502.3 14.3 %reduce-scatter.9.cloned.1.call-done = bf16[32,1024]{1,0:T(8,128)(2,1)} async-done(((bf16[128,1024]{1,0:T(8,128)(2,1)}), bf16[32,1024]{1,0:T(8,128)(2,1)}) %reduce-scatter.9.cloned.1.call-update) | async-done | bytes 65552 | tf_op jit(solution)/shard_map/reduce_scatter | solution.py:141
  517.5 22.1 %reduce-scatter.11.cloned.1.call-done = bf16[32,1024]{1,0:T(8,128)(2,1)} async-done(((bf16[128,1024]{1,0:T(8,128)(2,1)}), bf16[32,1024]{1,0:T(8,128)(2,1)}) %reduce-scatter.11.cloned.1.call-update) | async-done | bytes 65552 | tf_op jit(solution)/shard_map/reduce_scatter | solution.py:141
  543.6 40.6 %all-reduce.9 = (f32[32]{0:T(128)S(1)}, f32[32]{0:T(128)S(1)}) all-reduce(f32[32]{0:T(128)S(1)} %get-tuple-element.110, f32[32]{0:T(128)S(1)} %get-tuple-element.98), channel_id=1, replica_groups=mesh['segment'=2,'tensor'=4,'batch'=16] {'batch'}, use_global_device_ids=true, to_apply=%region_21.24 | all-reduce | flops 64 | bytes 512 | tf_op jit(solution)/shard_map/psum | solution.py:62
  584.3 12.3 %all_gather.21 = bf16[128,1024]{1,0:T(8,128)(2,1)S(1)} all-gather(bf16[32,1024]{1,0:T(8,128)(2,1)S(1)} %get-tuple-element.113), channel_id=1, replica_groups=mesh['segment'=2,'tensor'=4,'batch'=16] {'tensor'}, dimensions={0}, use_global_device_ids=true | all-gather | bytes 327680 | tf_op jit(solution)/shard_map/all_gather | solution.py:66
  597.9 4.0 fusion.22
  601.9 12.2 %all_gather.22 = bf16[128,1024]{1,0:T(8,128)(2,1)S(1)} all-gather(bf16[32,1024]{1,0:T(8,128)(2,1)S(1)} %get-tuple-element.112), channel_id=1, replica_groups=mesh['segment'=2,'tensor'=4,'batch'=16] {'tensor'}, dimensions={0}, use_global_device_ids=true | all-gather | bytes 327680 | tf_op jit(solution)/shard_map/all_gather | solution.py:66
  615.5 3.0 fusion.20
  619.8 88.3 %all-reduce.18 = (bf16[128,2560]{1,0:T(8,128)(2,1)}, bf16[128,2560]{1,0:T(8,128)(2,1)}) all-reduce(f32[128,2560]{1,0:T(8,128)S(1)} %pad_maximum_fusion.3, f32[128,2560]{1,0:T(8,128)} %pad_maximum_fusion.4), channel_id=8, replica_groups=mesh['segment'=2,'tensor'=4,'batch'=16] {'batch'}, use_global_device_ids=true, to_apply=%region_22.25.clone | all-reduce | flops 655360 | bytes 3932160
  713.1 6.3 collective-permute-done.62
  719.4 5.8 collective-permute-start.70
  727.3 5.3 collective-permute-start.71
  734.7 5.4 collective-permute-start.72
  742.3 5.3 collective-permute-start.73
  749.7 5.3 collective-permute-start.74
  757.0 5.3 collective-permute-start.75
  764.5 5.3 collective-permute-start.76
  773.1 4.8 collective-permute-done.54
  789.5 2.9 fusion.10
  795.1 15.0 %reduce-scatter.13.cloned.1.call-done = bf16[32,1024]{1,0:T(8,128)(2,1)} async-done(((bf16[128,1024]{1,0:T(8,128)(2,1)}), bf16[32,1024]{1,0:T(8,128)(2,1)}) %reduce-scatter.13.cloned.1.call-update) | async-done | bytes 65552 | tf_op jit(solution)/shard_map/reduce_scatter | solution.py:141
  811.0 21.9 %reduce-scatter.15.cloned.1.call-done = bf16[32,1024]{1,0:T(8,128)(2,1)} async-done(((bf16[128,1024]{1,0:T(8,128)(2,1)}), bf16[32,1024]{1,0:T(8,128)(2,1)}) %reduce-scatter.15.cloned.1.call-update) | async-done | bytes 65552 | tf_op jit(solution)/shard_map/reduce_scatter | solution.py:141
  836.0 40.6 %psum.47 = f32[32]{0:T(128)S(1)} all-reduce(f32[32]{0:T(128)S(1)} %fusion.94), channel_id=1, replica_groups=mesh['segment'=2,'tensor'=4,'batch'=16] {'batch'}, use_global_device_ids=true, to_apply=%region_33.36 | all-reduce | flops 32 | bytes 256 | tf_op jit(solution)/shard_map/psum | solution.py:62
  876.7 12.3 %all_gather.23 = bf16[128,1024]{1,0:T(8,128)(2,1)S(1)} all-gather(bf16[32,1024]{1,0:T(8,128)(2,1)S(1)} %fusion.96), channel_id=1, replica_groups=mesh['segment'=2,'tensor'=4,'batch'=16] {'tensor'}, dimensions={0}, use_global_device_ids=true | all-gather | bytes 327680 | tf_op jit(solution)/shard_map/all_gather | solution.py:66
  890.3 3.0 fusion.18
  893.4 82.2 %all-reduce.19 = bf16[128,2560]{1,0:T(8,128)(2,1)} all-reduce(f32[128,2560]{1,0:T(8,128)S(1)} %pad_maximum_fusion.5), channel_id=12, replica_groups=mesh['segment'=2,'tensor'=4,'batch'=16] {'batch'}, use_global_device_ids=true, to_apply=%region_34.37.clone | all-reduce | flops 327680 | bytes 1966080
  977.3 7.6 collective-permute-done.78
  984.9 5.3 collective-permute-start.86
  992.1 5.3 collective-permute-start.87
  999.4 5.3 collective-permute-start.88
  1006.6 5.3 collective-permute-start.89
  1013.8 5.3 collective-permute-start.90
  1021.1 5.3 collective-permute-start.91
  1028.3 5.4 collective-permute-start.92
  1036.4 2.9 fusion.6
  1041.9 19.6 %reduce-scatter.17.cloned.1.call-done = bf16[32,1024]{1,0:T(8,128)(2,1)} async-done(((bf16[128,1024]{1,0:T(8,128)(2,1)}), bf16[32,1024]{1,0:T(8,128)(2,1)}) %reduce-scatter.17.cloned.1.call-update) | async-done | bytes 65552 | tf_op jit(solution)/shard_map/reduce_scatter | solution.py:141
  (542 shorter events, 140.3 us)
Async XLA Ops:
  7.2 241.3 %reduce-scatter.7.cloned.1.call-start = ((), (), s32[]{:S(2)}) async-start(), calls=%async_computation.6 | async-start | bytes 327680 | tf_op jit(solution)/shard_map/reduce_scatter | solution.py:141
  170.9 7.4 collective-permute-start.8
  227.0 289.6 %reduce-scatter.9.cloned.1.call-start = ((), (), s32[]{:S(2)}) async-start(), calls=%async_computation.7 | async-start | bytes 327680 | tf_op jit(solution)/shard_map/reduce_scatter | solution.py:141
  419.4 7.4 collective-permute-start.31
  420.3 11.9 %collective-permute-start.16 = (bf16[8,2048]{1,0:T(8,128)(2,1)S(1)}, bf16[8,2048]{1,0:T(8,128)(2,1)S(1)}, u32[]{:S(2)}, u32[]{:S(2)}) collective-permute-start(bf16[8,2048]{1,0:T(8,128)(2,1)S(1)} %reshape.547), channel_id=1, source_target_pairs={{0,1},{1,2},{2,3},{3,4},{4,5},{5,6},{6,7},{7,8},{8,9},{9,10},{10,1... | collective-permute-start | bytes 98312 | tf_op jit(solution)/shard_map/ppermute | solution.py:121
  426.8 7.4 collective-permute-start.32
  426.8 7.5 collective-permute-start.39
  432.2 7.6 collective-permute-start.24
  432.2 8.1 collective-permute-start.17
  434.3 7.5 collective-permute-start.33
  434.3 7.6 collective-permute-start.40
  439.8 7.4 collective-permute-start.25
  440.3 7.4 collective-permute-start.18
  441.8 7.4 collective-permute-start.34
  441.9 7.4 collective-permute-start.41
  447.2 7.4 collective-permute-start.26
  449.2 7.4 collective-permute-start.35
  449.3 7.4 collective-permute-start.42
  454.5 7.4 collective-permute-start.27
  455.1 7.6 collective-permute-start.20
  456.6 7.6 collective-permute-start.36
  456.7 7.6 collective-permute-start.43
  461.9 7.6 collective-permute-start.28
  462.7 7.4 collective-permute-start.21
  464.2 7.4 collective-permute-start.37
  464.3 7.5 collective-permute-start.44
  469.5 7.5 collective-permute-start.29
  470.1 7.5 collective-permute-start.22
  471.6 7.5 collective-permute-start.38
  471.7 7.6 collective-permute-start.45
  477.0 17.4 %collective-permute-start.30 = (bf16[8,2048]{1,0:T(8,128)(2,1)}, bf16[8,2048]{1,0:T(8,128)(2,1)}, u32[]{:S(2)}, u32[]{:S(2)}) collective-permute-start(bf16[8,2048]{1,0:T(8,128)(2,1)} %collective-permute-done.29), channel_id=1, source_target_pairs={{1,0},{2,1},{3,2},{4,3},{5,4},{6,5},{7,6},{8,7},{9,8},{10,9},{11,1... | collective-permute-start | bytes 98312 | tf_op jit(solution)/shard_map/ppermute | solution.py:127
  477.6 7.6 collective-permute-start.23
  500.9 38.6 %reduce-scatter.11.cloned.1.call-start = ((), (), s32[]{:S(2)}) async-start(), calls=%async_computation.8 | async-start | bytes 327680 | tf_op jit(solution)/shard_map/reduce_scatter | solution.py:141
  501.6 308.5 %reduce-scatter.13.cloned.1.call-start = ((), (), s32[]{:S(2)}) async-start(), calls=%async_computation.9 | async-start | bytes 327680 | tf_op jit(solution)/shard_map/reduce_scatter | solution.py:141
  713.0 12.3 %collective-permute-start.47 = (bf16[8,2048]{1,0:T(8,128)(2,1)S(1)}, bf16[8,2048]{1,0:T(8,128)(2,1)S(1)}, u32[]{:S(2)}, u32[]{:S(2)}) collective-permute-start(bf16[8,2048]{1,0:T(8,128)(2,1)S(1)} %reshape.556), channel_id=1, source_target_pairs={{0,1},{1,2},{2,3},{3,4},{4,5},{5,6},{6,7},{7,8},{8,9},{9,10},{10,1... | collective-permute-start | bytes 98312 | tf_op jit(solution)/shard_map/ppermute | solution.py:121
  719.4 7.8 collective-permute-start.63
  719.4 7.9 collective-permute-start.70
  725.3 7.9 collective-permute-start.48
  727.3 7.4 collective-permute-start.64
  732.6 7.5 collective-permute-start.56
  733.2 7.4 collective-permute-start.49
  734.6 7.5 collective-permute-start.65
  734.7 7.5 collective-permute-start.72
  740.1 7.4 collective-permute-start.57
  740.6 7.4 collective-permute-start.50
  742.2 7.4 collective-permute-start.66
  742.3 7.4 collective-permute-start.73
  747.5 7.4 collective-permute-start.58
  748.0 7.4 collective-permute-start.51
  749.6 7.4 collective-permute-start.67
  749.7 7.4 collective-permute-start.74
  754.9 7.4 collective-permute-start.59
  755.4 7.4 collective-permute-start.52
  757.0 7.4 collective-permute-start.68
  757.0 7.4 collective-permute-start.75
  762.3 7.5 collective-permute-start.60
  762.7 7.5 collective-permute-start.53
  764.4 7.7 collective-permute-start.69
  764.5 7.7 collective-permute-start.76
  769.8 18.2 %collective-permute-start.61 = (bf16[8,2048]{1,0:T(8,128)(2,1)}, bf16[8,2048]{1,0:T(8,128)(2,1)}, u32[]{:S(2)}, u32[]{:S(2)}) collective-permute-start(bf16[8,2048]{1,0:T(8,128)(2,1)} %collective-permute-done.60), channel_id=1, source_target_pairs={{1,0},{2,1},{3,2},{4,3},{5,4},{6,5},{7,6},{8,7},{9,8},{10,9},{11,1... | collective-permute-start | bytes 98312 | tf_op jit(solution)/shard_map/ppermute | solution.py:127
  770.3 7.7 collective-permute-start.54
  794.4 38.4 %reduce-scatter.15.cloned.1.call-start = ((), (), s32[]{:S(2)}) async-start(), calls=%async_computation.10 | async-start | bytes 327680 | tf_op jit(solution)/shard_map/reduce_scatter | solution.py:141
  795.0 266.5 %reduce-scatter.17.cloned.1.call-start = ((), (), s32[]{:S(2)}) async-start(), calls=%async_computation.11 | async-start | bytes 327680 | tf_op jit(solution)/shard_map/reduce_scatter | solution.py:141
  977.3 7.6 collective-permute-start.78
  (82 other events, 2215.4 us)
Sparse Core Ops, SparseCore 0:
  227.1 21.2 reduce-scatter.6
  501.0 15.5 reduce-scatter.8
  519.0 20.5 reduce-scatter.10
  794.6 15.4 reduce-scatter.12
  812.3 20.5 reduce-scatter.14
  1041.3 20.1 reduce-scatter.16
